TPU v7x, 32 devices: a whole 2x2x4 slice. The times are simulated.
32 devices in a mesh: pipe: 4 (over z), sx: 4 (over y, x), sy: 2 (over core).
Axes of the slice: x: 2, y: 2, z: 4, core: 2. Of those that a mesh axis runs over, the one named last changes fastest.
Arguments:
- segment_inputs: bfloat16 [4, 1, 4, 2, 512, 128], P('pipe', None, 'sx', 'sy'), may hold values from -6 to 6
- out_cotangent: bfloat16 [1, 4, 2, 512, 128], P(None, 'sx', 'sy'), may hold values from -6 to 6
- neighbours: int32 [1, 4, 2, 1, 27], P(None, 'sx', 'sy'), may hold values from 0 to 1, as said below
- block_counts: int32 [1, 4, 2], P(None, 'sx', 'sy'), may hold values from 1 to 1, as said below
- norm_gain: float32 [4, 128], P('pipe'), may hold values from 0.1 to 1.9
- kernel: bfloat16 [4, 3456, 128], P('pipe', 'sx'), may hold values from -0.109375 to 0.109375
Outputs:
- grad_inputs: bfloat16 [4, 1, 4, 2, 512, 128], P('pipe', None, 'sx', 'sy')
- kernel_grad: float32 [4, 3456, 128], P('pipe', 'sx')
Inputs may be any that keep to these rules, and one draw needn't show every extreme that they name: `neighbours`: entry [m, a, b, s, (i + 1) * 9 + (j + 1) * 3 + (k + 1)], i, j, k in -1..1, is the slot in the list of slab (a + i, b + j) of the occupied block lying i, j, k blocks from slot s of slab (a, b) along x, y, z, or 1 where that block is not occupied, the slab is off the grid, or slot s is padding; it never names a padding slot. `block_counts`: slots 0 to count - 1 of a slab's list hold its occupied blocks; later slots are padding.
All inputs are finite; a program needn't handle non-finite values.
Results may differ from a plain program's by a relative error of at most 0.014.
Values may be sent and summed in bfloat16 or wider, within the bound.
No kernel may reach another device: no remote copies, remote signals or barrier semaphores. Data moves between devices by JAX's collectives and lax.ppermute only.
A program may use at most 64 MiB of HBM per device.

v0:
```python
import jax
import jax.numpy as jnp
from jax import lax
from jax.sharding import PartitionSpec as P

OFFSETS = (-1, 0, 1)


def source_range(offset):
    if offset < 0:
        return slice(7, 8)
    if offset > 0:
        return slice(0, 1)
    return slice(0, 8)


def activate(values, gain_row):
    floats = values.astype(jnp.float32)
    square = jnp.mean(floats * floats, axis=-1, keepdims=True)
    return jax.nn.silu(floats * lax.rsqrt(square + 1e-06) * gain_row)


def with_blank(blocks_in):
    return jnp.concatenate([blocks_in, jnp.zeros_like(blocks_in)], axis=0)


def face_piece(cube, shift_x, shift_y):
    return cube[:, source_range(shift_x), source_range(shift_y)]


def directions():
    return [(sx, sy) for sx in OFFSETS for sy in OFFSETS if (sx, sy) != (0, 0)]


def assemble(centre, received, table):
    slabs_x = []
    for shift_x in OFFSETS:
        rows_y = []
        for shift_y in OFFSETS:
            column = (shift_x + 1) * 3 + (shift_y + 1)
            source = with_blank(
                centre if (shift_x, shift_y) == (0, 0) else received[shift_x, shift_y]
            )
            parts_z = []
            for shift_z in OFFSETS:
                direction = column * 3 + shift_z + 1
                picked = source[table[:, direction]]
                parts_z.append(picked[:, :, :, source_range(shift_z), :])
            rows_y.append(jnp.concatenate(parts_z, axis=3))
        slabs_x.append(jnp.concatenate(rows_y, axis=2))
    return jnp.concatenate(slabs_x, axis=1)


def exchange(cube, axes, sizes, pipe_step):
    received = {}
    for shift_x, shift_y in directions():
        piece = face_piece(cube, shift_x, shift_y)
        route = []
        if pipe_step:
            n_pipe, n_x, n_y = sizes
            for p in range(pipe_step, n_pipe):
                for a in range(n_x):
                    for b in range(n_y):
                        ta, tb = (a - shift_x, b - shift_y)
                        if 0 <= ta < n_x and 0 <= tb < n_y:
                            route.append(
                                ((p * n_x + a) * n_y + b, ((p - pipe_step) * n_x + ta) * n_y + tb)
                            )
        else:
            n_x, n_y = sizes
            for a in range(n_x):
                for b in range(n_y):
                    ta, tb = (a - shift_x, b - shift_y)
                    if 0 <= ta < n_x and 0 <= tb < n_y:
                        route.append((a * n_y + b, ta * n_y + tb))
        received[shift_x, shift_y] = lax.ppermute(piece, axes, route)
    return received


def columns(padded, rows, sign):
    taps = []
    for tap_x in OFFSETS:
        for tap_y in OFFSETS:
            for tap_z in OFFSETS:
                taps.append(
                    padded[
                        :,
                        1 + sign * tap_x : 9 + sign * tap_x,
                        1 + sign * tap_y : 9 + sign * tap_y,
                        1 + sign * tap_z : 9 + sign * tap_z,
                        :,
                    ]
                )
    stacked = jnp.stack(taps, axis=-2)
    return stacked.reshape(rows, len(taps) * padded.shape[-1])


def finish_grad(values, grad_live, live_now, grad_act, gain_row):
    _, pullback = jax.vjp(lambda floats: activate(floats, gain_row), values.astype(jnp.float32))
    (through,) = pullback(grad_act)
    summed = grad_live.astype(jnp.float32) + through
    result = jnp.where(live_now[:, None], summed, jnp.zeros_like(summed))
    return result.astype(jnp.bfloat16)


def shards(segment_inputs, out_cotangent, neighbours, block_counts, norm_gain, kernel):
    n_pipe = lax.axis_size("pipe")
    n_x = lax.axis_size("sx")
    n_y = lax.axis_size("sy")
    segment_place = lax.axis_index("pipe")
    micro_count = segment_inputs.shape[1]
    row_count = segment_inputs.shape[4]
    channels = segment_inputs.shape[5]
    blocks = row_count // 512
    taps = 27
    weights = lax.all_gather(kernel[0], "sx", axis=0, tiled=True)
    flipped = (
        weights.reshape(taps, channels, channels)
        .transpose(0, 2, 1)
        .reshape(taps * channels, channels)
    )
    gain_row = norm_gain[0]
    inputs = segment_inputs[0, :, 0, 0]
    cotangent = out_cotangent[:, 0, 0]
    tables = neighbours[:, 0, 0]
    slot_ids = jnp.arange(row_count, dtype=jnp.int32) // 512
    live_rows = slot_ids[None, :] < block_counts[:, 0, 0][:, None]

    def cube(values):
        return values.reshape(blocks, 8, 8, 8, channels)

    grads_out = []
    kernel_total = jnp.zeros((taps * channels, channels), jnp.float32)
    for micro in range(micro_count):
        table = tables[micro]
        live_now = live_rows[micro]
        values = inputs[micro]
        activation = activate(values, gain_row).astype(jnp.bfloat16)
        start = cotangent[micro]
        start = jnp.where(live_now[:, None], start, jnp.zeros_like(start))
        both = jnp.concatenate([cube(activation), cube(start)], axis=-1)
        got = exchange(both, ("sx", "sy"), (n_x, n_y), 0)
        act_pad = assemble(cube(activation), {k: v[..., :channels] for k, v in got.items()}, table)
        act_cols = columns(act_pad, row_count, 1)
        centre = start
        received = {k: v[..., channels:] for k, v in got.items()}
        kept_dy = start
        kept_grad = jnp.zeros((row_count, channels), jnp.bfloat16)
        for tick in range(n_pipe):
            active = segment_place == n_pipe - 1 - tick
            grad_pad = assemble(cube(centre), received, table)
            grad_act = jnp.dot(
                columns(grad_pad, row_count, -1), flipped, preferred_element_type=jnp.float32
            )
            result = finish_grad(values, centre, live_now, grad_act, gain_row)
            kept_dy = jnp.where(active, centre, kept_dy)
            kept_grad = jnp.where(active, result, kept_grad)
            if tick < n_pipe - 1:
                down = [(p, p - 1) for p in range(1, n_pipe)]
                centre = lax.ppermute(result, "pipe", down)
                received = exchange(cube(result), ("pipe", "sx", "sy"), (n_pipe, n_x, n_y), 1)
        kernel_total = kernel_total + lax.dot_general(
            act_cols, kept_dy, (((0,), (0,)), ((), ())), preferred_element_type=jnp.float32
        )
        grads_out.append(kept_grad)
    grad_store = jnp.stack(grads_out)
    norm_scale = float(n_x * n_y * micro_count * row_count) ** (-0.5)
    kernel_term = kernel_total * norm_scale
    shard_rows = kernel.shape[1]
    summed = lax.psum(kernel_term.astype(jnp.bfloat16), "sy").astype(jnp.float32)
    kernel_share = lax.psum_scatter(
        lax.slice_in_dim(summed, 0, shard_rows * n_x, axis=0).astype(jnp.bfloat16),
        "sx",
        scatter_dimension=0,
        tiled=True,
    ).astype(jnp.float32)
    return (grad_store[None, :, None, None], kernel_share[None])


def solution(mesh):
    return jax.shard_map(
        shards,
        mesh=mesh,
        in_specs=(
            P("pipe", None, "sx", "sy", None, None),
            P(None, "sx", "sy", None, None),
            P(None, "sx", "sy", None, None),
            P(None, "sx", "sy"),
            P("pipe", None),
            P("pipe", "sx", None),
        ),
        out_specs=(P("pipe", None, "sx", "sy", None, None), P("pipe", "sx", None)),
        check_vma=False,
    )
```

profile of v0, /device:TPU:0, one launch (start us, length us, event | category | flops | bytes accessed | tf_op | source)
XLA Modules:
  0.0 277.4 jit_solution(7714859741776979580)
XLA Ops:
  7.2 1.1 fusion.13
  9.1 1.0 broadcast_select_fusion
  10.1 1.1 multiply_convert_fusion
  11.2 1.3 collective-permute-start.4
  12.5 4.8 %collective-permute-start.6 = (bf16[1,1,8,8,256]{4,3,2,1,0:T(8,128)(2,1)S(1)}, bf16[1,1,8,8,256]{4,3,2,1,0:T(8,128)(2,1)S(1)}, u32[]{:S(2)}, u32[]{:S(2)}) collective-permute-start(bf16[1,1,8,8,256]{4,3,2,1,0:T(8,128)(2,1)S(1)} %get-tuple-element.1491), channel_id=1, source_target_pairs={{0,2},{1,3},{2,4},{3,5},{4,6},{5,7},{8,10},{9,11},{10,12},{11,13},... | collective-permute-start | bytes 98312 | tf_op jit(solution)/shard_map/ppermute | solution.py:76
  17.4 1.3 collective-permute-start.3
  19.4 1.3 collective-permute-start.1
  20.7 2.1 fusion.89
  36.6 1.6 fusion.90
  46.1 19.6 %all-gather = bf16[1,3456,128]{2,1,0:T(8,128)(2,1)S(1)} all-gather(bf16[1,864,128]{2,1,0:T(8,128)(2,1)} %param.11), channel_id=2, replica_groups=mesh['pipe'=4,'sx'=4,'sy'=2] {'sx'}, dimensions={1}, use_global_device_ids=true | all-gather | bytes 1105920 | tf_op jit(solution)/shard_map/all_gather | solution.py:116
  80.3 1.3 copy.138
  96.8 1.6 collective-permute-start
  99.2 6.2 %collective-permute-start.5 = (bf16[1,1,1,8,256]{4,3,2,1,0:T(8,128)(2,1)S(1)}, bf16[1,1,1,8,256]{4,3,2,1,0:T(8,128)(2,1)S(1)}, u32[]{:S(2)}, u32[]{:S(2)}) collective-permute-start(bf16[1,1,1,8,256]{4,3,2,1,0:T(8,128)(2,1)S(1)} %get-tuple-element.1487), channel_id=1, source_target_pairs={{0,3},{2,5},{4,7},{8,11},{10,13},{12,15},{16,19},{18,21},{20,23},{... | collective-permute-start | bytes 12296 | tf_op jit(solution)/shard_map/ppermute | solution.py:76
  105.4 1.3 collective-permute-done.5
  110.0 1.2 fusion.35
  111.5 1.3 collective-permute-start.8
  113.0 1.3 collective-permute-start.13
  114.3 1.3 collective-permute-start.12
  116.3 1.3 collective-permute-start.10
  122.8 0.8 collective-permute-start.15
  126.9 1.2 fusion.36
  128.5 1.3 collective-permute-start.17
  129.8 1.3 collective-permute-start.22
  131.1 1.3 collective-permute-start.21
  133.1 1.3 collective-permute-start.19
  134.4 15.8 %collective-permute-done.22 = bf16[1,1,1,8,128]{4,3,2,1,0:T(8,128)(2,1)S(1)} collective-permute-done((bf16[1,1,1,8,128]{4,3,2,1,0:T(8,128)(2,1)S(1)}, bf16[1,1,1,8,128]{4,3,2,1,0:T(8,128)(2,1)S(1)}, u32[]{:S(2)}, u32[]{:S(2)}) %collective-permute-start.22) | collective-permute-done | bytes 2080 | tf_op jit(solution)/shard_map/ppermute | solution.py:76
  156.2 1.2 fusion.37
  157.7 1.3 collective-permute-start.26
  159.1 1.3 collective-permute-start.31
  160.4 1.3 collective-permute-start.30
  162.4 1.3 collective-permute-start.28
  163.7 19.4 %collective-permute-done.31 = bf16[1,1,1,8,128]{4,3,2,1,0:T(8,128)(2,1)S(1)} collective-permute-done((bf16[1,1,1,8,128]{4,3,2,1,0:T(8,128)(2,1)S(1)}, bf16[1,1,1,8,128]{4,3,2,1,0:T(8,128)(2,1)S(1)}, u32[]{:S(2)}, u32[]{:S(2)}) %collective-permute-start.31) | collective-permute-done | bytes 2080 | tf_op jit(solution)/shard_map/ppermute | solution.py:76
  185.2 0.9 collective-permute-start.33
  191.5 0.7 constant_dynamic-update-slice_fusion.101
  192.2 0.7 constant_dynamic-update-slice_fusion.100
  192.9 0.7 constant_dynamic-update-slice_fusion.99
  195.8 0.7 constant_dynamic-update-slice_fusion.95
  197.2 0.7 constant_dynamic-update-slice_fusion.93
  200.4 0.7 constant_dynamic-update-slice_fusion.89
  202.5 2.2 fusion
  204.7 0.8 constant_dynamic-update-slice_fusion.86
  205.5 0.7 constant_dynamic-update-slice_fusion.85
  207.7 0.7 constant_dynamic-update-slice_fusion.82
  209.1 3.2 %fusion.38 = (f32[512]{0:T(512)S(1)}, f32[512,128]{1,0:T(8,128)S(1)}) fusion(bf16[1,1,1,1,512,128]{5,4,3,2,1,0:T(8,128)(2,1)S(1)} %copy-done, f32[128]{0:T(128)S(1)} %bitcast.970, f32[512]{0:T(512)S(1)} %fusion.70, bf16[512,3456]{1,0:T(8,128)(2,1)} %bitcast.281, bf16[3456,128]{1,0:T(8,128)(2,1)S(1)} %bitcast.950), kind=kOutput, calls=%fused_computation.238 | convolution fusion | flops 453967360 | bytes 4821504 | tf_op jit(solution)/shard_map/dot_general | solution.py:152
  212.3 36.1 %reduce-scatter.2.cloned.1.call-done = bf16[864,128]{1,0:T(8,128)(2,1)} async-done(((bf16[3456,128]{1,0:T(8,128)(2,1)}), bf16[864,128]{1,0:T(8,128)(2,1)}) %reduce-scatter.2.cloned.1.call-update) | async-done | bytes 221200 | tf_op jit(solution)/shard_map/reduce_scatter | solution.py:171
  248.4 1.0 fusion.40
  249.4 19.4 %all-reduce.47.cloned.1.call-done = bf16[864,128]{1,0:T(8,128)(2,1)} async-done(((bf16[864,128]{1,0:T(8,128)(2,1)}), bf16[864,128]{1,0:T(8,128)(2,1)}) %all-reduce.47.cloned.1.call-update) | async-done | bytes 221200 | tf_op jit(solution)/shard_map/psum | solution.py:170
  268.8 1.7 bitcast_convert_fusion
  (330 shorter events, 37.6 us)
Async XLA Ops:
  7.2 241.2 %reduce-scatter.2.cloned.1.call-start = ((), (), s32[]{:S(2)}) async-start(), calls=%async_computation.1 | async-start | bytes 1105920 | tf_op jit(solution)/shard_map/reduce_scatter | solution.py:171
  11.2 85.6 %collective-permute-start.4 = (bf16[1,1,1,8,256]{4,3,2,1,0:T(8,128)(2,1)S(1)}, bf16[1,1,1,8,256]{4,3,2,1,0:T(8,128)(2,1)S(1)}, u32[]{:S(2)}, u32[]{:S(2)}) collective-permute-start(bf16[1,1,1,8,256]{4,3,2,1,0:T(8,128)(2,1)S(1)} %get-tuple-element.1489), channel_id=1, source_target_pairs={{3,0},{5,2},{7,4},{11,8},{13,10},{15,12},{19,16},{21,18},{23,20},{... | collective-permute-start | bytes 12296 | tf_op jit(solution)/shard_map/ppermute | solution.py:76
  12.5 94.6 %collective-permute-start.6 = (bf16[1,1,8,8,256]{4,3,2,1,0:T(8,128)(2,1)S(1)}, bf16[1,1,8,8,256]{4,3,2,1,0:T(8,128)(2,1)S(1)}, u32[]{:S(2)}, u32[]{:S(2)}) collective-permute-start(bf16[1,1,8,8,256]{4,3,2,1,0:T(8,128)(2,1)S(1)} %get-tuple-element.1491), channel_id=1, source_target_pairs={{0,2},{1,3},{2,4},{3,5},{4,6},{5,7},{8,10},{9,11},{10,12},{11,13},... | collective-permute-start | bytes 98312 | tf_op jit(solution)/shard_map/ppermute | solution.py:76
  17.4 89.5 %collective-permute-start.3 = (bf16[1,1,8,8,256]{4,3,2,1,0:T(8,128)(2,1)S(1)}, bf16[1,1,8,8,256]{4,3,2,1,0:T(8,128)(2,1)S(1)}, u32[]{:S(2)}, u32[]{:S(2)}) collective-permute-start(bf16[1,1,8,8,256]{4,3,2,1,0:T(8,128)(2,1)S(1)} %get-tuple-element.1492), channel_id=1, source_target_pairs={{2,0},{3,1},{4,2},{5,3},{6,4},{7,5},{10,8},{11,9},{12,10},{13,11},... | collective-permute-start | bytes 98312 | tf_op jit(solution)/shard_map/ppermute | solution.py:76
  18.7 79.8 %collective-permute-start.2 = (bf16[1,1,1,8,256]{4,3,2,1,0:T(8,128)(2,1)S(1)}, bf16[1,1,1,8,256]{4,3,2,1,0:T(8,128)(2,1)S(1)}, u32[]{:S(2)}, u32[]{:S(2)}) collective-permute-start(bf16[1,1,1,8,256]{4,3,2,1,0:T(8,128)(2,1)S(1)} %get-tuple-element.1488), channel_id=1, source_target_pairs={{2,1},{4,3},{6,5},{10,9},{12,11},{14,13},{18,17},{20,19},{22,21},{... | collective-permute-start | bytes 12296 | tf_op jit(solution)/shard_map/ppermute | solution.py:76
  19.4 87.6 %collective-permute-start.1 = (bf16[1,8,1,8,256]{4,3,2,1,0:T(8,128)(2,1)S(1)}, bf16[1,8,1,8,256]{4,3,2,1,0:T(8,128)(2,1)S(1)}, u32[]{:S(2)}, u32[]{:S(2)}) collective-permute-start(bf16[1,8,1,8,256]{4,3,2,1,0:T(8,128)(2,1)S(1)} %get-tuple-element.1494), channel_id=1, source_target_pairs={{1,0},{3,2},{5,4},{7,6},{9,8},{11,10},{13,12},{15,14},{17,16},{19,... | collective-permute-start | bytes 98312 | tf_op jit(solution)/shard_map/ppermute | solution.py:76
  96.8 10.2 %collective-permute-start = (bf16[1,8,1,8,256]{4,3,2,1,0:T(8,128)(2,1)S(1)}, bf16[1,8,1,8,256]{4,3,2,1,0:T(8,128)(2,1)S(1)}, u32[]{:S(2)}, u32[]{:S(2)}) collective-permute-start(bf16[1,8,1,8,256]{4,3,2,1,0:T(8,128)(2,1)S(1)} %get-tuple-element.1493), channel_id=1, source_target_pairs={{0,1},{2,3},{4,5},{6,7},{8,9},{10,11},{12,13},{14,15},{16,17},{18,... | collective-permute-start | bytes 98312 | tf_op jit(solution)/shard_map/ppermute | solution.py:76
  98.5 0.7 collective-permute-start.7
  99.2 7.5 %collective-permute-start.5 = (bf16[1,1,1,8,256]{4,3,2,1,0:T(8,128)(2,1)S(1)}, bf16[1,1,1,8,256]{4,3,2,1,0:T(8,128)(2,1)S(1)}, u32[]{:S(2)}, u32[]{:S(2)}) collective-permute-start(bf16[1,1,1,8,256]{4,3,2,1,0:T(8,128)(2,1)S(1)} %get-tuple-element.1487), channel_id=1, source_target_pairs={{0,3},{2,5},{4,7},{8,11},{10,13},{12,15},{16,19},{18,21},{20,23},{... | collective-permute-start | bytes 12296 | tf_op jit(solution)/shard_map/ppermute | solution.py:76
  108.0 2.0 copy-start
  108.0 2.0 copy-start.2
  109.7 1.5 copy-start.1
  111.5 12.6 %collective-permute-start.8 = (bf16[512,128]{1,0:T(8,128)(2,1)S(1)}, bf16[512,128]{1,0:T(8,128)(2,1)S(1)}, u32[]{:S(2)}, u32[]{:S(2)}) collective-permute-start(bf16[512,128]{1,0:T(8,128)(2,1)S(1)} %fusion.3), channel_id=1, source_target_pairs={{8,0},{16,8},{24,16},{9,1},{17,9},{25,17},{10,2},{18,10},{26,18},{... | collective-permute-start | bytes 393224 | tf_op jit(solution)/shard_map/ppermute | solution.py:160
  113.0 7.7 %collective-permute-start.13 = (bf16[1,1,1,8,128]{4,3,2,1,0:T(8,128)(2,1)S(1)}, bf16[1,1,1,8,128]{4,3,2,1,0:T(8,128)(2,1)S(1)}, u32[]{:S(2)}, u32[]{:S(2)}) collective-permute-start(bf16[1,1,1,8,128]{4,3,2,1,0:T(8,128)(2,1)S(1)} %get-tuple-element.1529), channel_id=1, source_target_pairs={{11,0},{13,2},{15,4},{19,8},{21,10},{23,12},{27,16},{29,18},{31,20}} | collective-permute-start | bytes 6152 | tf_op jit(solution)/shard_map/ppermute | solution.py:76
  114.3 9.5 %collective-permute-start.12 = (bf16[1,1,8,8,128]{4,3,2,1,0:T(8,128)(2,1)S(1)}, bf16[1,1,8,8,128]{4,3,2,1,0:T(8,128)(2,1)S(1)}, u32[]{:S(2)}, u32[]{:S(2)}) collective-permute-start(bf16[1,1,8,8,128]{4,3,2,1,0:T(8,128)(2,1)S(1)} %get-tuple-element.1532), channel_id=1, source_target_pairs={{10,0},{11,1},{12,2},{13,3},{14,4},{15,5},{18,8},{19,9},{20,10},{2... | collective-permute-start | bytes 49160 | tf_op jit(solution)/shard_map/ppermute | solution.py:76
  115.6 5.8 %collective-permute-start.11 = (bf16[1,1,1,8,128]{4,3,2,1,0:T(8,128)(2,1)S(1)}, bf16[1,1,1,8,128]{4,3,2,1,0:T(8,128)(2,1)S(1)}, u32[]{:S(2)}, u32[]{:S(2)}) collective-permute-start(bf16[1,1,1,8,128]{4,3,2,1,0:T(8,128)(2,1)S(1)} %get-tuple-element.1530), channel_id=1, source_target_pairs={{10,1},{12,3},{14,5},{18,9},{20,11},{22,13},{26,17},{28,19},{30,21}} | collective-permute-start | bytes 6152 | tf_op jit(solution)/shard_map/ppermute | solution.py:76
  116.3 7.6 %collective-permute-start.10 = (bf16[1,8,1,8,128]{4,3,2,1,0:T(8,128)(2,1)S(1)}, bf16[1,8,1,8,128]{4,3,2,1,0:T(8,128)(2,1)S(1)}, u32[]{:S(2)}, u32[]{:S(2)}) collective-permute-start(bf16[1,8,1,8,128]{4,3,2,1,0:T(8,128)(2,1)S(1)} %get-tuple-element.1534), channel_id=1, source_target_pairs={{9,0},{11,2},{13,4},{15,6},{17,8},{19,10},{21,12},{23,14},{25,16},... | collective-permute-start | bytes 49160 | tf_op jit(solution)/shard_map/ppermute | solution.py:76
  120.7 3.3 %collective-permute-start.9 = (bf16[1,8,1,8,128]{4,3,2,1,0:T(8,128)(2,1)S(1)}, bf16[1,8,1,8,128]{4,3,2,1,0:T(8,128)(2,1)S(1)}, u32[]{:S(2)}, u32[]{:S(2)}) collective-permute-start(bf16[1,8,1,8,128]{4,3,2,1,0:T(8,128)(2,1)S(1)} %get-tuple-element.1533), channel_id=1, source_target_pairs={{8,1},{10,3},{12,5},{14,7},{16,9},{18,11},{20,13},{22,15},{24,17},... | collective-permute-start | bytes 49160 | tf_op jit(solution)/shard_map/ppermute | solution.py:76
  121.4 0.7 collective-permute-start.16
  122.1 0.7 collective-permute-start.14
  122.8 1.2 collective-permute-start.15
  128.5 24.9 %collective-permute-start.17 = (bf16[512,128]{1,0:T(8,128)(2,1)S(1)}, bf16[512,128]{1,0:T(8,128)(2,1)S(1)}, u32[]{:S(2)}, u32[]{:S(2)}) collective-permute-start(bf16[512,128]{1,0:T(8,128)(2,1)S(1)} %fusion.6), channel_id=1, source_target_pairs={{8,0},{16,8},{24,16},{9,1},{17,9},{25,17},{10,2},{18,10},{26,18},{... | collective-permute-start | bytes 393224 | tf_op jit(solution)/shard_map/ppermute | solution.py:160
  129.8 20.3 %collective-permute-start.22 = (bf16[1,1,1,8,128]{4,3,2,1,0:T(8,128)(2,1)S(1)}, bf16[1,1,1,8,128]{4,3,2,1,0:T(8,128)(2,1)S(1)}, u32[]{:S(2)}, u32[]{:S(2)}) collective-permute-start(bf16[1,1,1,8,128]{4,3,2,1,0:T(8,128)(2,1)S(1)} %get-tuple-element.1519), channel_id=1, source_target_pairs={{11,0},{13,2},{15,4},{19,8},{21,10},{23,12},{27,16},{29,18},{31,20}} | collective-permute-start | bytes 6152 | tf_op jit(solution)/shard_map/ppermute | solution.py:76
  131.1 22.0 %collective-permute-start.21 = (bf16[1,1,8,8,128]{4,3,2,1,0:T(8,128)(2,1)S(1)}, bf16[1,1,8,8,128]{4,3,2,1,0:T(8,128)(2,1)S(1)}, u32[]{:S(2)}, u32[]{:S(2)}) collective-permute-start(bf16[1,1,8,8,128]{4,3,2,1,0:T(8,128)(2,1)S(1)} %get-tuple-element.1522), channel_id=1, source_target_pairs={{10,0},{11,1},{12,2},{13,3},{14,4},{15,5},{18,8},{19,9},{20,10},{2... | collective-permute-start | bytes 49160 | tf_op jit(solution)/shard_map/ppermute | solution.py:76
  132.4 18.4 %collective-permute-start.20 = (bf16[1,1,1,8,128]{4,3,2,1,0:T(8,128)(2,1)S(1)}, bf16[1,1,1,8,128]{4,3,2,1,0:T(8,128)(2,1)S(1)}, u32[]{:S(2)}, u32[]{:S(2)}) collective-permute-start(bf16[1,1,1,8,128]{4,3,2,1,0:T(8,128)(2,1)S(1)} %get-tuple-element.1520), channel_id=1, source_target_pairs={{10,1},{12,3},{14,5},{18,9},{20,11},{22,13},{26,17},{28,19},{30,21}} | collective-permute-start | bytes 6152 | tf_op jit(solution)/shard_map/ppermute | solution.py:76
  133.1 20.1 %collective-permute-start.19 = (bf16[1,8,1,8,128]{4,3,2,1,0:T(8,128)(2,1)S(1)}, bf16[1,8,1,8,128]{4,3,2,1,0:T(8,128)(2,1)S(1)}, u32[]{:S(2)}, u32[]{:S(2)}) collective-permute-start(bf16[1,8,1,8,128]{4,3,2,1,0:T(8,128)(2,1)S(1)} %get-tuple-element.1524), channel_id=1, source_target_pairs={{9,0},{11,2},{13,4},{15,6},{17,8},{19,10},{21,12},{23,14},{25,16},... | collective-permute-start | bytes 49160 | tf_op jit(solution)/shard_map/ppermute | solution.py:76
  150.1 3.1 %collective-permute-start.18 = (bf16[1,8,1,8,128]{4,3,2,1,0:T(8,128)(2,1)S(1)}, bf16[1,8,1,8,128]{4,3,2,1,0:T(8,128)(2,1)S(1)}, u32[]{:S(2)}, u32[]{:S(2)}) collective-permute-start(bf16[1,8,1,8,128]{4,3,2,1,0:T(8,128)(2,1)S(1)} %get-tuple-element.1523), channel_id=1, source_target_pairs={{8,1},{10,3},{12,5},{14,7},{16,9},{18,11},{20,13},{22,15},{24,17},... | collective-permute-start | bytes 49160 | tf_op jit(solution)/shard_map/ppermute | solution.py:76
  150.8 0.7 collective-permute-start.25
  151.6 0.7 collective-permute-start.23
  152.3 1.0 collective-permute-start.24
  157.7 28.8 %collective-permute-start.26 = (bf16[512,128]{1,0:T(8,128)(2,1)S(1)}, bf16[512,128]{1,0:T(8,128)(2,1)S(1)}, u32[]{:S(2)}, u32[]{:S(2)}) collective-permute-start(bf16[512,128]{1,0:T(8,128)(2,1)S(1)} %fusion.9), channel_id=1, source_target_pairs={{8,0},{16,8},{24,16},{9,1},{17,9},{25,17},{10,2},{18,10},{26,18},{... | collective-permute-start | bytes 393224 | tf_op jit(solution)/shard_map/ppermute | solution.py:160
  159.1 24.0 %collective-permute-start.31 = (bf16[1,1,1,8,128]{4,3,2,1,0:T(8,128)(2,1)S(1)}, bf16[1,1,1,8,128]{4,3,2,1,0:T(8,128)(2,1)S(1)}, u32[]{:S(2)}, u32[]{:S(2)}) collective-permute-start(bf16[1,1,1,8,128]{4,3,2,1,0:T(8,128)(2,1)S(1)} %get-tuple-element.1509), channel_id=1, source_target_pairs={{11,0},{13,2},{15,4},{19,8},{21,10},{23,12},{27,16},{29,18},{31,20}} | collective-permute-start | bytes 6152 | tf_op jit(solution)/shard_map/ppermute | solution.py:76
  160.4 25.8 %collective-permute-start.30 = (bf16[1,1,8,8,128]{4,3,2,1,0:T(8,128)(2,1)S(1)}, bf16[1,1,8,8,128]{4,3,2,1,0:T(8,128)(2,1)S(1)}, u32[]{:S(2)}, u32[]{:S(2)}) collective-permute-start(bf16[1,1,8,8,128]{4,3,2,1,0:T(8,128)(2,1)S(1)} %get-tuple-element.1512), channel_id=1, source_target_pairs={{10,0},{11,1},{12,2},{13,3},{14,4},{15,5},{18,8},{19,9},{20,10},{2... | collective-permute-start | bytes 49160 | tf_op jit(solution)/shard_map/ppermute | solution.py:76
  161.7 22.0 %collective-permute-start.29 = (bf16[1,1,1,8,128]{4,3,2,1,0:T(8,128)(2,1)S(1)}, bf16[1,1,1,8,128]{4,3,2,1,0:T(8,128)(2,1)S(1)}, u32[]{:S(2)}, u32[]{:S(2)}) collective-permute-start(bf16[1,1,1,8,128]{4,3,2,1,0:T(8,128)(2,1)S(1)} %get-tuple-element.1510), channel_id=1, source_target_pairs={{10,1},{12,3},{14,5},{18,9},{20,11},{22,13},{26,17},{28,19},{30,21}} | collective-permute-start | bytes 6152 | tf_op jit(solution)/shard_map/ppermute | solution.py:76
  162.4 23.9 %collective-permute-start.28 = (bf16[1,8,1,8,128]{4,3,2,1,0:T(8,128)(2,1)S(1)}, bf16[1,8,1,8,128]{4,3,2,1,0:T(8,128)(2,1)S(1)}, u32[]{:S(2)}, u32[]{:S(2)}) collective-permute-start(bf16[1,8,1,8,128]{4,3,2,1,0:T(8,128)(2,1)S(1)} %get-tuple-element.1514), channel_id=1, source_target_pairs={{9,0},{11,2},{13,4},{15,6},{17,8},{19,10},{21,12},{23,14},{25,16},... | collective-permute-start | bytes 49160 | tf_op jit(solution)/shard_map/ppermute | solution.py:76
  183.0 3.3 %collective-permute-start.27 = (bf16[1,8,1,8,128]{4,3,2,1,0:T(8,128)(2,1)S(1)}, bf16[1,8,1,8,128]{4,3,2,1,0:T(8,128)(2,1)S(1)}, u32[]{:S(2)}, u32[]{:S(2)}) collective-permute-start(bf16[1,8,1,8,128]{4,3,2,1,0:T(8,128)(2,1)S(1)} %get-tuple-element.1513), channel_id=1, source_target_pairs={{8,1},{10,3},{12,5},{14,7},{16,9},{18,11},{20,13},{22,15},{24,17},... | collective-permute-start | bytes 49160 | tf_op jit(solution)/shard_map/ppermute | solution.py:76
  183.7 0.7 collective-permute-start.34
  184.5 0.7 collective-permute-start.32
  185.2 1.2 collective-permute-start.33
  204.7 64.1 %all-reduce.47.cloned.1.call-start = ((), (), s32[]{:S(2)}) async-start(), calls=%async_computation.2 | async-start | bytes 442368 | tf_op jit(solution)/shard_map/psum | solution.py:170
Sparse Core Ops, SparseCore 0:
  204.8 43.4 reduce-scatter.1
  250.7 18.0 all-reduce.46
where the time goes:
time: 279 us; the launch traced here: 277 us
  waiting for transfers between devices  92 us (33%)
  between operations  68 us (24%)
  starting transfers between devices  43.7 us (16%)
  local copies, waits for them, and re-layouts  31.8 us (11%)
  blocking collectives  19.6 us (7%)
  other arithmetic  13.3 us (5%)
  matrix products  8.99 us (3%)
    ppermute x32, starting transfers between devices, exchange(): received[shift_x, shift_y] = lax.ppermute(piece, axes, route)  39.7 us
    ppermute x32, waiting for transfers between devices, exchange(): received[shift_x, shift_y] = lax.ppermute(piece, axes, route)  36.5 us
    reduce_scatter x1, waiting for transfers between devices, shards(): lax.psum_scatter(lax.slice_in_dim(summed, 0, shard_rows * n_x, axis=0).as...  36.1 us
    unnamed x126, local copies, waits for them, and re-layouts  22.9 us
    all_gather x1, blocking collectives, shards(): weights = lax.all_gather(kernel[0], 'sx', axis=0, tiled=True)  19.6 us
    psum x1, waiting for transfers between devices, shards(): lax.psum(kernel_term.astype(jnp.bfloat16), 'sy').astype(jnp.float32)  19.4 us
    dot_general x4, matrix products, shards(): jnp.dot(columns(grad_pad, row_count, -1), flipped, preferred_element_type...  6.82 us
  transfers between devices with their start and end apart: 37, of which 5 were waited for; matrix products, arithmetic and copies ran while one was open for 7% of the time, Pallas kernels for 0%

commit v1 on v0

--- a/solution.py
+++ b/solution.py
@@ -1,9 +1,17 @@
+import functools
 import jax
 import jax.numpy as jnp
 from jax import lax
 from jax.sharding import PartitionSpec as P
 
 OFFSETS = (-1, 0, 1)
+
+
+def keep_up_side_here(u_in, bus_axis):
+    return jnp.sum(jax.lax.all_gather(u_in, bus_axis), axis=0)
+
+
+remake_the_ticks = functools.partial(keep_up_side_here, bus_axis="sy")
 
 
 def source_range(offset):
@@ -167,7 +175,7 @@
     norm_scale = float(n_x * n_y * micro_count * row_count) ** (-0.5)
     kernel_term = kernel_total * norm_scale
     shard_rows = kernel.shape[1]
-    summed = lax.psum(kernel_term.astype(jnp.bfloat16), "sy").astype(jnp.float32)
+    summed = remake_the_ticks(kernel_term.astype(jnp.bfloat16)).astype(jnp.float32)
     kernel_share = lax.psum_scatter(
         lax.slice_in_dim(summed, 0, shard_rows * n_x, axis=0).astype(jnp.bfloat16),
         "sx",

time: 279 us -> 269 us (0.964)
  waiting for transfers between devices: 92 us -> 78.5 us
  other arithmetic: 13.3 us -> 16.2 us
    all_gather x0 -> x1, waiting for transfers between devices: none -> 21 us  [keep_up_side_here(): return jnp.sum(jax.lax.all_gather(u_in, bus_axis), axis=0)]
    psum x1 -> x0, waiting for transfers between devices: 19.4 us -> none  [shards(): lax.psum(kernel_term.astype(jnp.bfloat16), 'sy').astype(jnp.float32)]
    reduce_scatter x1, waiting for transfers between devices: 36.1 us -> 21 us  [shards(): lax.psum_scatter(lax.slice_in_dim(summed, 0, shard_rows * n_x, axis=0).as...]
    reduce_sum x0 -> x1, other arithmetic: none -> 2.97 us  [keep_up_side_here(): return jnp.sum(jax.lax.all_gather(u_in, bus_axis), axis=0)]
  transfers between devices with their start and end apart: 37 -> 37, of which waited for: 5 -> 5; matrix products, arithmetic and copies ran while one was open for 7% -> 9% of each run, Pallas kernels for 0% -> 0%
where the time goes in v1:
time: 269 us; the launch traced here: 267 us
  waiting for transfers between devices  78.5 us (29%)
  between operations  68 us (25%)
  starting transfers between devices  43.7 us (16%)
  local copies, waits for them, and re-layouts  31.8 us (12%)
  blocking collectives  19.6 us (7%)
  other arithmetic  16.2 us (6%)
  matrix products  8.98 us (3%)
    ppermute x32, starting transfers between devices, exchange(): received[shift_x, shift_y] = lax.ppermute(piece, axes, route)  39.7 us
    ppermute x32, waiting for transfers between devices, exchange(): received[shift_x, shift_y] = lax.ppermute(piece, axes, route)  36.5 us
    unnamed x126, local copies, waits for them, and re-layouts  22.9 us
    all_gather x1, waiting for transfers between devices, keep_up_side_here(): return jnp.sum(jax.lax.all_gather(u_in, bus_axis), axis=0)  21 us
    reduce_scatter x1, waiting for transfers between devices, shards(): lax.psum_scatter(lax.slice_in_dim(summed, 0, shard_rows * n_x, axis=0).as...  21 us
    all_gather x1, blocking collectives, shards(): weights = lax.all_gather(kernel[0], 'sx', axis=0, tiled=True)  19.6 us
    dot_general x4, matrix products, shards(): jnp.dot(columns(grad_pad, row_count, -1), flipped, preferred_element_type...  6.83 us
  transfers between devices with their start and end apart: 37, of which 5 were waited for; matrix products, arithmetic and copies ran while one was open for 9% of the time, Pallas kernels for 0%

profile of v1, /device:TPU:0, one launch (start us, length us, event | category | flops | bytes accessed | tf_op | source)
XLA Modules:
  0.0 266.8 jit_solution(5664243946565253871)
XLA Ops:
  7.2 1.1 fusion.13
  9.1 1.0 broadcast_select_fusion
  10.1 1.1 multiply_convert_fusion
  11.2 1.3 collective-permute-start.4
  12.5 4.8 %collective-permute-start.6 = (bf16[1,1,8,8,256]{4,3,2,1,0:T(8,128)(2,1)S(1)}, bf16[1,1,8,8,256]{4,3,2,1,0:T(8,128)(2,1)S(1)}, u32[]{:S(2)}, u32[]{:S(2)}) collective-permute-start(bf16[1,1,8,8,256]{4,3,2,1,0:T(8,128)(2,1)S(1)} %get-tuple-element.1491), channel_id=1, source_target_pairs={{0,2},{1,3},{2,4},{3,5},{4,6},{5,7},{8,10},{9,11},{10,12},{11,13},... | collective-permute-start | bytes 98312 | tf_op jit(solution)/shard_map/ppermute | solution.py:84
  17.4 1.3 collective-permute-start.3
  19.4 1.3 collective-permute-start.1
  20.7 2.1 fusion.89
  36.6 1.6 fusion.90
  46.1 19.6 %all-gather = bf16[1,3456,128]{2,1,0:T(8,128)(2,1)S(1)} all-gather(bf16[1,864,128]{2,1,0:T(8,128)(2,1)} %param.11), channel_id=2, replica_groups=mesh['pipe'=4,'sx'=4,'sy'=2] {'sx'}, dimensions={1}, use_global_device_ids=true | all-gather | bytes 1105920 | tf_op jit(solution)/shard_map/all_gather | solution.py:124
  80.3 1.3 copy.138
  96.8 1.6 collective-permute-start
  99.2 6.2 %collective-permute-start.5 = (bf16[1,1,1,8,256]{4,3,2,1,0:T(8,128)(2,1)S(1)}, bf16[1,1,1,8,256]{4,3,2,1,0:T(8,128)(2,1)S(1)}, u32[]{:S(2)}, u32[]{:S(2)}) collective-permute-start(bf16[1,1,1,8,256]{4,3,2,1,0:T(8,128)(2,1)S(1)} %get-tuple-element.1487), channel_id=1, source_target_pairs={{0,3},{2,5},{4,7},{8,11},{10,13},{12,15},{16,19},{18,21},{20,23},{... | collective-permute-start | bytes 12296 | tf_op jit(solution)/shard_map/ppermute | solution.py:84
  105.4 1.3 collective-permute-done.5
  110.0 1.2 fusion.35
  111.5 1.3 collective-permute-start.8
  113.0 1.3 collective-permute-start.13
  114.3 1.3 collective-permute-start.12
  116.3 1.3 collective-permute-start.10
  122.8 0.8 collective-permute-start.15
  126.9 1.2 fusion.36
  128.5 1.3 collective-permute-start.17
  129.8 1.3 collective-permute-start.22
  131.1 1.3 collective-permute-start.21
  133.1 1.3 collective-permute-start.19
  134.4 15.8 %collective-permute-done.22 = bf16[1,1,1,8,128]{4,3,2,1,0:T(8,128)(2,1)S(1)} collective-permute-done((bf16[1,1,1,8,128]{4,3,2,1,0:T(8,128)(2,1)S(1)}, bf16[1,1,1,8,128]{4,3,2,1,0:T(8,128)(2,1)S(1)}, u32[]{:S(2)}, u32[]{:S(2)}) %collective-permute-start.22) | collective-permute-done | bytes 2080 | tf_op jit(solution)/shard_map/ppermute | solution.py:84
  156.2 1.2 fusion.37
  157.8 1.3 collective-permute-start.26
  159.1 1.3 collective-permute-start.31
  160.4 1.3 collective-permute-start.30
  162.4 1.3 collective-permute-start.28
  163.7 19.4 %collective-permute-done.31 = bf16[1,1,1,8,128]{4,3,2,1,0:T(8,128)(2,1)S(1)} collective-permute-done((bf16[1,1,1,8,128]{4,3,2,1,0:T(8,128)(2,1)S(1)}, bf16[1,1,1,8,128]{4,3,2,1,0:T(8,128)(2,1)S(1)}, u32[]{:S(2)}, u32[]{:S(2)}) %collective-permute-start.31) | collective-permute-done | bytes 2080 | tf_op jit(solution)/shard_map/ppermute | solution.py:84
  185.2 0.9 collective-permute-start.33
  191.5 0.7 constant_dynamic-update-slice_fusion.101
  192.2 0.7 constant_dynamic-update-slice_fusion.100
  192.9 0.7 constant_dynamic-update-slice_fusion.99
  195.8 0.7 constant_dynamic-update-slice_fusion.95
  197.2 0.7 constant_dynamic-update-slice_fusion.93
  198.0 2.1 fusion
  204.7 0.8 constant_dynamic-update-slice_fusion.86
  205.5 0.7 constant_dynamic-update-slice_fusion.85
  206.2 21.0 %all-gather.4.cloned.1.call-done = bf16[6912,128]{1,0:T(8,128)(2,1)} async-done(((bf16[3456,128]{1,0:T(8,128)(2,1)}), bf16[6912,128]{1,0:T(8,128)(2,1)}) %all-gather.4.cloned.1.call-update) | async-done | bytes 1769488 | tf_op jit(solution)/shard_map/all_gather | solution.py:11
  227.2 3.0 %reduce_sum.65 = bf16[3456,128]{1,0:T(8,128)(2,1)} reduce(bf16[2,3456,128]{2,1,0:T(8,128)(2,1)} %bitcast.948, bf16[]{:T(256)} %constant.59.clone.1), dimensions={0}, to_apply=%region_5.6 | reduce | flops 442368 | bytes 2654210 | tf_op jit(solution)/shard_map/reduce_sum | solution.py:11
  231.6 0.7 constant_dynamic-update-slice_fusion.82
  233.1 3.2 %fusion.38 = (f32[512]{0:T(512)S(1)}, f32[512,128]{1,0:T(8,128)S(1)}) fusion(bf16[1,1,1,1,512,128]{5,4,3,2,1,0:T(8,128)(2,1)S(1)} %copy-done, f32[128]{0:T(128)S(1)} %bitcast.972, f32[512]{0:T(512)S(1)} %fusion.70, bf16[512,3456]{1,0:T(8,128)(2,1)} %bitcast.281, bf16[3456,128]{1,0:T(8,128)(2,1)S(1)} %bitcast.952), kind=kOutput, calls=%fused_computation.238 | convolution fusion | flops 453967360 | bytes 4821504 | tf_op jit(solution)/shard_map/dot_general | solution.py:160
  236.3 1.0 fusion.40
  237.3 21.0 %reduce-scatter.2.cloned.1.call-done = bf16[864,128]{1,0:T(8,128)(2,1)} async-done(((bf16[3456,128]{1,0:T(8,128)(2,1)}), bf16[864,128]{1,0:T(8,128)(2,1)}) %reduce-scatter.2.cloned.1.call-update) | async-done | bytes 221200 | tf_op jit(solution)/shard_map/reduce_scatter | solution.py:179
  258.2 1.7 bitcast_convert_fusion
  (331 shorter events, 38.4 us)
Async XLA Ops:
  7.2 220.1 %all-gather.4.cloned.1.call-start = ((), (), s32[]{:S(2)}) async-start(), calls=%async_computation.2 | async-start | bytes 2654208 | tf_op jit(solution)/shard_map/all_gather | solution.py:11
  11.2 85.6 %collective-permute-start.4 = (bf16[1,1,1,8,256]{4,3,2,1,0:T(8,128)(2,1)S(1)}, bf16[1,1,1,8,256]{4,3,2,1,0:T(8,128)(2,1)S(1)}, u32[]{:S(2)}, u32[]{:S(2)}) collective-permute-start(bf16[1,1,1,8,256]{4,3,2,1,0:T(8,128)(2,1)S(1)} %get-tuple-element.1489), channel_id=1, source_target_pairs={{3,0},{5,2},{7,4},{11,8},{13,10},{15,12},{19,16},{21,18},{23,20},{... | collective-permute-start | bytes 12296 | tf_op jit(solution)/shard_map/ppermute | solution.py:84
  12.5 94.6 %collective-permute-start.6 = (bf16[1,1,8,8,256]{4,3,2,1,0:T(8,128)(2,1)S(1)}, bf16[1,1,8,8,256]{4,3,2,1,0:T(8,128)(2,1)S(1)}, u32[]{:S(2)}, u32[]{:S(2)}) collective-permute-start(bf16[1,1,8,8,256]{4,3,2,1,0:T(8,128)(2,1)S(1)} %get-tuple-element.1491), channel_id=1, source_target_pairs={{0,2},{1,3},{2,4},{3,5},{4,6},{5,7},{8,10},{9,11},{10,12},{11,13},... | collective-permute-start | bytes 98312 | tf_op jit(solution)/shard_map/ppermute | solution.py:84
  17.4 89.5 %collective-permute-start.3 = (bf16[1,1,8,8,256]{4,3,2,1,0:T(8,128)(2,1)S(1)}, bf16[1,1,8,8,256]{4,3,2,1,0:T(8,128)(2,1)S(1)}, u32[]{:S(2)}, u32[]{:S(2)}) collective-permute-start(bf16[1,1,8,8,256]{4,3,2,1,0:T(8,128)(2,1)S(1)} %get-tuple-element.1492), channel_id=1, source_target_pairs={{2,0},{3,1},{4,2},{5,3},{6,4},{7,5},{10,8},{11,9},{12,10},{13,11},... | collective-permute-start | bytes 98312 | tf_op jit(solution)/shard_map/ppermute | solution.py:84
  18.7 79.8 %collective-permute-start.2 = (bf16[1,1,1,8,256]{4,3,2,1,0:T(8,128)(2,1)S(1)}, bf16[1,1,1,8,256]{4,3,2,1,0:T(8,128)(2,1)S(1)}, u32[]{:S(2)}, u32[]{:S(2)}) collective-permute-start(bf16[1,1,1,8,256]{4,3,2,1,0:T(8,128)(2,1)S(1)} %get-tuple-element.1488), channel_id=1, source_target_pairs={{2,1},{4,3},{6,5},{10,9},{12,11},{14,13},{18,17},{20,19},{22,21},{... | collective-permute-start | bytes 12296 | tf_op jit(solution)/shard_map/ppermute | solution.py:84
  19.4 87.6 %collective-permute-start.1 = (bf16[1,8,1,8,256]{4,3,2,1,0:T(8,128)(2,1)S(1)}, bf16[1,8,1,8,256]{4,3,2,1,0:T(8,128)(2,1)S(1)}, u32[]{:S(2)}, u32[]{:S(2)}) collective-permute-start(bf16[1,8,1,8,256]{4,3,2,1,0:T(8,128)(2,1)S(1)} %get-tuple-element.1494), channel_id=1, source_target_pairs={{1,0},{3,2},{5,4},{7,6},{9,8},{11,10},{13,12},{15,14},{17,16},{19,... | collective-permute-start | bytes 98312 | tf_op jit(solution)/shard_map/ppermute | solution.py:84
  96.8 10.2 %collective-permute-start = (bf16[1,8,1,8,256]{4,3,2,1,0:T(8,128)(2,1)S(1)}, bf16[1,8,1,8,256]{4,3,2,1,0:T(8,128)(2,1)S(1)}, u32[]{:S(2)}, u32[]{:S(2)}) collective-permute-start(bf16[1,8,1,8,256]{4,3,2,1,0:T(8,128)(2,1)S(1)} %get-tuple-element.1493), channel_id=1, source_target_pairs={{0,1},{2,3},{4,5},{6,7},{8,9},{10,11},{12,13},{14,15},{16,17},{18,... | collective-permute-start | bytes 98312 | tf_op jit(solution)/shard_map/ppermute | solution.py:84
  98.5 0.7 collective-permute-start.7
  99.2 7.5 %collective-permute-start.5 = (bf16[1,1,1,8,256]{4,3,2,1,0:T(8,128)(2,1)S(1)}, bf16[1,1,1,8,256]{4,3,2,1,0:T(8,128)(2,1)S(1)}, u32[]{:S(2)}, u32[]{:S(2)}) collective-permute-start(bf16[1,1,1,8,256]{4,3,2,1,0:T(8,128)(2,1)S(1)} %get-tuple-element.1487), channel_id=1, source_target_pairs={{0,3},{2,5},{4,7},{8,11},{10,13},{12,15},{16,19},{18,21},{20,23},{... | collective-permute-start | bytes 12296 | tf_op jit(solution)/shard_map/ppermute | solution.py:84
  108.0 2.0 copy-start
  108.0 2.0 copy-start.2
  109.7 1.5 copy-start.1
  111.5 12.6 %collective-permute-start.8 = (bf16[512,128]{1,0:T(8,128)(2,1)S(1)}, bf16[512,128]{1,0:T(8,128)(2,1)S(1)}, u32[]{:S(2)}, u32[]{:S(2)}) collective-permute-start(bf16[512,128]{1,0:T(8,128)(2,1)S(1)} %fusion.3), channel_id=1, source_target_pairs={{8,0},{16,8},{24,16},{9,1},{17,9},{25,17},{10,2},{18,10},{26,18},{... | collective-permute-start | bytes 393224 | tf_op jit(solution)/shard_map/ppermute | solution.py:168
  113.0 7.7 %collective-permute-start.13 = (bf16[1,1,1,8,128]{4,3,2,1,0:T(8,128)(2,1)S(1)}, bf16[1,1,1,8,128]{4,3,2,1,0:T(8,128)(2,1)S(1)}, u32[]{:S(2)}, u32[]{:S(2)}) collective-permute-start(bf16[1,1,1,8,128]{4,3,2,1,0:T(8,128)(2,1)S(1)} %get-tuple-element.1529), channel_id=1, source_target_pairs={{11,0},{13,2},{15,4},{19,8},{21,10},{23,12},{27,16},{29,18},{31,20}} | collective-permute-start | bytes 6152 | tf_op jit(solution)/shard_map/ppermute | solution.py:84
  114.3 9.5 %collective-permute-start.12 = (bf16[1,1,8,8,128]{4,3,2,1,0:T(8,128)(2,1)S(1)}, bf16[1,1,8,8,128]{4,3,2,1,0:T(8,128)(2,1)S(1)}, u32[]{:S(2)}, u32[]{:S(2)}) collective-permute-start(bf16[1,1,8,8,128]{4,3,2,1,0:T(8,128)(2,1)S(1)} %get-tuple-element.1532), channel_id=1, source_target_pairs={{10,0},{11,1},{12,2},{13,3},{14,4},{15,5},{18,8},{19,9},{20,10},{2... | collective-permute-start | bytes 49160 | tf_op jit(solution)/shard_map/ppermute | solution.py:84
  115.6 5.8 %collective-permute-start.11 = (bf16[1,1,1,8,128]{4,3,2,1,0:T(8,128)(2,1)S(1)}, bf16[1,1,1,8,128]{4,3,2,1,0:T(8,128)(2,1)S(1)}, u32[]{:S(2)}, u32[]{:S(2)}) collective-permute-start(bf16[1,1,1,8,128]{4,3,2,1,0:T(8,128)(2,1)S(1)} %get-tuple-element.1530), channel_id=1, source_target_pairs={{10,1},{12,3},{14,5},{18,9},{20,11},{22,13},{26,17},{28,19},{30,21}} | collective-permute-start | bytes 6152 | tf_op jit(solution)/shard_map/ppermute | solution.py:84
  116.3 7.6 %collective-permute-start.10 = (bf16[1,8,1,8,128]{4,3,2,1,0:T(8,128)(2,1)S(1)}, bf16[1,8,1,8,128]{4,3,2,1,0:T(8,128)(2,1)S(1)}, u32[]{:S(2)}, u32[]{:S(2)}) collective-permute-start(bf16[1,8,1,8,128]{4,3,2,1,0:T(8,128)(2,1)S(1)} %get-tuple-element.1534), channel_id=1, source_target_pairs={{9,0},{11,2},{13,4},{15,6},{17,8},{19,10},{21,12},{23,14},{25,16},... | collective-permute-start | bytes 49160 | tf_op jit(solution)/shard_map/ppermute | solution.py:84
  120.7 3.3 %collective-permute-start.9 = (bf16[1,8,1,8,128]{4,3,2,1,0:T(8,128)(2,1)S(1)}, bf16[1,8,1,8,128]{4,3,2,1,0:T(8,128)(2,1)S(1)}, u32[]{:S(2)}, u32[]{:S(2)}) collective-permute-start(bf16[1,8,1,8,128]{4,3,2,1,0:T(8,128)(2,1)S(1)} %get-tuple-element.1533), channel_id=1, source_target_pairs={{8,1},{10,3},{12,5},{14,7},{16,9},{18,11},{20,13},{22,15},{24,17},... | collective-permute-start | bytes 49160 | tf_op jit(solution)/shard_map/ppermute | solution.py:84
  121.4 0.7 collective-permute-start.16
  122.1 0.7 collective-permute-start.14
  122.8 1.2 collective-permute-start.15
  128.5 24.9 %collective-permute-start.17 = (bf16[512,128]{1,0:T(8,128)(2,1)S(1)}, bf16[512,128]{1,0:T(8,128)(2,1)S(1)}, u32[]{:S(2)}, u32[]{:S(2)}) collective-permute-start(bf16[512,128]{1,0:T(8,128)(2,1)S(1)} %fusion.6), channel_id=1, source_target_pairs={{8,0},{16,8},{24,16},{9,1},{17,9},{25,17},{10,2},{18,10},{26,18},{... | collective-permute-start | bytes 393224 | tf_op jit(solution)/shard_map/ppermute | solution.py:168
  129.8 20.3 %collective-permute-start.22 = (bf16[1,1,1,8,128]{4,3,2,1,0:T(8,128)(2,1)S(1)}, bf16[1,1,1,8,128]{4,3,2,1,0:T(8,128)(2,1)S(1)}, u32[]{:S(2)}, u32[]{:S(2)}) collective-permute-start(bf16[1,1,1,8,128]{4,3,2,1,0:T(8,128)(2,1)S(1)} %get-tuple-element.1519), channel_id=1, source_target_pairs={{11,0},{13,2},{15,4},{19,8},{21,10},{23,12},{27,16},{29,18},{31,20}} | collective-permute-start | bytes 6152 | tf_op jit(solution)/shard_map/ppermute | solution.py:84
  131.1 22.0 %collective-permute-start.21 = (bf16[1,1,8,8,128]{4,3,2,1,0:T(8,128)(2,1)S(1)}, bf16[1,1,8,8,128]{4,3,2,1,0:T(8,128)(2,1)S(1)}, u32[]{:S(2)}, u32[]{:S(2)}) collective-permute-start(bf16[1,1,8,8,128]{4,3,2,1,0:T(8,128)(2,1)S(1)} %get-tuple-element.1522), channel_id=1, source_target_pairs={{10,0},{11,1},{12,2},{13,3},{14,4},{15,5},{18,8},{19,9},{20,10},{2... | collective-permute-start | bytes 49160 | tf_op jit(solution)/shard_map/ppermute | solution.py:84
  132.4 18.4 %collective-permute-start.20 = (bf16[1,1,1,8,128]{4,3,2,1,0:T(8,128)(2,1)S(1)}, bf16[1,1,1,8,128]{4,3,2,1,0:T(8,128)(2,1)S(1)}, u32[]{:S(2)}, u32[]{:S(2)}) collective-permute-start(bf16[1,1,1,8,128]{4,3,2,1,0:T(8,128)(2,1)S(1)} %get-tuple-element.1520), channel_id=1, source_target_pairs={{10,1},{12,3},{14,5},{18,9},{20,11},{22,13},{26,17},{28,19},{30,21}} | collective-permute-start | bytes 6152 | tf_op jit(solution)/shard_map/ppermute | solution.py:84
  133.1 20.1 %collective-permute-start.19 = (bf16[1,8,1,8,128]{4,3,2,1,0:T(8,128)(2,1)S(1)}, bf16[1,8,1,8,128]{4,3,2,1,0:T(8,128)(2,1)S(1)}, u32[]{:S(2)}, u32[]{:S(2)}) collective-permute-start(bf16[1,8,1,8,128]{4,3,2,1,0:T(8,128)(2,1)S(1)} %get-tuple-element.1524), channel_id=1, source_target_pairs={{9,0},{11,2},{13,4},{15,6},{17,8},{19,10},{21,12},{23,14},{25,16},... | collective-permute-start | bytes 49160 | tf_op jit(solution)/shard_map/ppermute | solution.py:84
  150.1 3.1 %collective-permute-start.18 = (bf16[1,8,1,8,128]{4,3,2,1,0:T(8,128)(2,1)S(1)}, bf16[1,8,1,8,128]{4,3,2,1,0:T(8,128)(2,1)S(1)}, u32[]{:S(2)}, u32[]{:S(2)}) collective-permute-start(bf16[1,8,1,8,128]{4,3,2,1,0:T(8,128)(2,1)S(1)} %get-tuple-element.1523), channel_id=1, source_target_pairs={{8,1},{10,3},{12,5},{14,7},{16,9},{18,11},{20,13},{22,15},{24,17},... | collective-permute-start | bytes 49160 | tf_op jit(solution)/shard_map/ppermute | solution.py:84
  150.8 0.7 collective-permute-start.25
  151.6 0.7 collective-permute-start.23
  152.3 1.0 collective-permute-start.24
  157.8 28.8 %collective-permute-start.26 = (bf16[512,128]{1,0:T(8,128)(2,1)S(1)}, bf16[512,128]{1,0:T(8,128)(2,1)S(1)}, u32[]{:S(2)}, u32[]{:S(2)}) collective-permute-start(bf16[512,128]{1,0:T(8,128)(2,1)S(1)} %fusion.9), channel_id=1, source_target_pairs={{8,0},{16,8},{24,16},{9,1},{17,9},{25,17},{10,2},{18,10},{26,18},{... | collective-permute-start | bytes 393224 | tf_op jit(solution)/shard_map/ppermute | solution.py:168
  159.1 24.0 %collective-permute-start.31 = (bf16[1,1,1,8,128]{4,3,2,1,0:T(8,128)(2,1)S(1)}, bf16[1,1,1,8,128]{4,3,2,1,0:T(8,128)(2,1)S(1)}, u32[]{:S(2)}, u32[]{:S(2)}) collective-permute-start(bf16[1,1,1,8,128]{4,3,2,1,0:T(8,128)(2,1)S(1)} %get-tuple-element.1509), channel_id=1, source_target_pairs={{11,0},{13,2},{15,4},{19,8},{21,10},{23,12},{27,16},{29,18},{31,20}} | collective-permute-start | bytes 6152 | tf_op jit(solution)/shard_map/ppermute | solution.py:84
  160.4 25.8 %collective-permute-start.30 = (bf16[1,1,8,8,128]{4,3,2,1,0:T(8,128)(2,1)S(1)}, bf16[1,1,8,8,128]{4,3,2,1,0:T(8,128)(2,1)S(1)}, u32[]{:S(2)}, u32[]{:S(2)}) collective-permute-start(bf16[1,1,8,8,128]{4,3,2,1,0:T(8,128)(2,1)S(1)} %get-tuple-element.1512), channel_id=1, source_target_pairs={{10,0},{11,1},{12,2},{13,3},{14,4},{15,5},{18,8},{19,9},{20,10},{2... | collective-permute-start | bytes 49160 | tf_op jit(solution)/shard_map/ppermute | solution.py:84
  161.7 22.0 %collective-permute-start.29 = (bf16[1,1,1,8,128]{4,3,2,1,0:T(8,128)(2,1)S(1)}, bf16[1,1,1,8,128]{4,3,2,1,0:T(8,128)(2,1)S(1)}, u32[]{:S(2)}, u32[]{:S(2)}) collective-permute-start(bf16[1,1,1,8,128]{4,3,2,1,0:T(8,128)(2,1)S(1)} %get-tuple-element.1510), channel_id=1, source_target_pairs={{10,1},{12,3},{14,5},{18,9},{20,11},{22,13},{26,17},{28,19},{30,21}} | collective-permute-start | bytes 6152 | tf_op jit(solution)/shard_map/ppermute | solution.py:84
  162.4 23.9 %collective-permute-start.28 = (bf16[1,8,1,8,128]{4,3,2,1,0:T(8,128)(2,1)S(1)}, bf16[1,8,1,8,128]{4,3,2,1,0:T(8,128)(2,1)S(1)}, u32[]{:S(2)}, u32[]{:S(2)}) collective-permute-start(bf16[1,8,1,8,128]{4,3,2,1,0:T(8,128)(2,1)S(1)} %get-tuple-element.1514), channel_id=1, source_target_pairs={{9,0},{11,2},{13,4},{15,6},{17,8},{19,10},{21,12},{23,14},{25,16},... | collective-permute-start | bytes 49160 | tf_op jit(solution)/shard_map/ppermute | solution.py:84
  183.0 3.3 %collective-permute-start.27 = (bf16[1,8,1,8,128]{4,3,2,1,0:T(8,128)(2,1)S(1)}, bf16[1,8,1,8,128]{4,3,2,1,0:T(8,128)(2,1)S(1)}, u32[]{:S(2)}, u32[]{:S(2)}) collective-permute-start(bf16[1,8,1,8,128]{4,3,2,1,0:T(8,128)(2,1)S(1)} %get-tuple-element.1513), channel_id=1, source_target_pairs={{8,1},{10,3},{12,5},{14,7},{16,9},{18,11},{20,13},{22,15},{24,17},... | collective-permute-start | bytes 49160 | tf_op jit(solution)/shard_map/ppermute | solution.py:84
  183.7 0.7 collective-permute-start.34
  184.5 0.7 collective-permute-start.32
  185.2 1.2 collective-permute-start.33
  200.2 58.1 %reduce-scatter.2.cloned.1.call-start = ((), (), s32[]{:S(2)}) async-start(), calls=%async_computation.1 | async-start | bytes 1105920 | tf_op jit(solution)/shard_map/reduce_scatter | solution.py:179
Sparse Core Ops, SparseCore 0:
  200.3 26.8 all-gather.3
  230.3 27.8 reduce-scatter.1
